TPU v7x, 32 devices: a whole 2x2x4 slice. The times are simulated.
32 devices in a mesh: grp: 2 (over x), wide: 16 (over z, y, core).
Axes of the slice: x: 2, y: 2, z: 4, core: 2. Of those that a mesh axis runs over, the one named last changes fastest.
Arguments:
- query_maps: bfloat16 [4096, 1024], P(('grp', 'wide')), parts along dimension 0
- source_maps: bfloat16 [4096, 1024], P(('grp', 'wide')), parts along dimension 0
- hubs: int32 [8], P('grp'), parts along dimension 0, may hold values from 0 to 15, as said below
- pick: int32 [32, 2], P(('grp', 'wide')), parts along dimension 0, may hold values from 0 to 3, all different within a row
- weight_first: bfloat16 [16, 1, 3, 3, 3, 3], replicated, may hold values from -0.625 to 0.625
- bias_first: float32 [16], replicated, may hold values from -0.6 to 0.6
- weight_second: bfloat16 [1, 16, 3, 3, 3, 3], replicated, may hold values from -0.15625 to 0.15625
- bias_second: float32 [1], replicated, may hold values from 0 to 0.2
Outputs:
- consensus: float32 [32, 2, 128, 128], P(('grp', 'wide')), parts along dimension 0
There are 2 independent parts, one for each index of `grp`. A program takes and returns all parts, laid end to end along the dimension named above; an argument that names none is the same for every part. Nothing has to cross between parts.
Inputs may be any that keep to these rules, and one draw needn't show every extreme that they name: `hubs`: distinct photo indices of the batch.
All inputs are finite; a program needn't handle non-finite values.
Results may differ from a plain program's by a relative error of at most 0.0063.
Values may be sent and summed in bfloat16 or wider, within the bound.
No kernel may reach another device: no remote copies, remote signals or barrier semaphores. Data moves between devices by JAX's collectives and lax.ppermute only.
A program may use at most 64 MiB of HBM per device.

v0:
```python
import jax
import jax.numpy as jnp
from jax import lax
from jax.sharding import PartitionSpec as P

HQ = 4
WQ = 32
HUBS = 4


def spread(value, axis, source):
    kept = jnp.where(lax.axis_index(axis) == source, value, 0).astype(value.dtype)
    return lax.psum(kept, axis)


def conv_volume(volume, kernel):
    padded = jnp.pad(volume, ((1, 1), (0, 0), (0, 0), (0, 0), (0, 0)))
    height = volume.shape[0]
    result = None
    for offset in range(3):
        term = lax.conv_general_dilated(
            padded[offset : offset + height],
            kernel[:, :, offset],
            (1, 1, 1),
            [(1, 1), (1, 1), (1, 1)],
            preferred_element_type=jnp.float32,
        )
        result = term if result is None else result + term
    return result


def consensus_net(matrix, weight_first, bias_first, weight_second, bias_second):
    cells = matrix.shape[0]
    volume = matrix.reshape(HQ, WQ, HQ, WQ)[:, None]
    preact = conv_volume(volume, weight_first) + bias_first[None, :, None, None, None]
    hidden = jax.nn.relu(preact).astype(jnp.bfloat16)
    result = jax.nn.relu(
        conv_volume(hidden, weight_second) + bias_second[None, :, None, None, None]
    )
    return result.reshape(cells, cells)


def scaled_corr(query, sources):
    query_f = query.astype(jnp.float32)
    sources_f = sources.astype(jnp.float32)
    query_rms = jnp.sqrt(jnp.mean(query_f * query_f, axis=-1) + 1e-06)
    source_rms = jnp.sqrt(jnp.mean(sources_f * sources_f, axis=-1) + 1e-06)
    inner = jnp.einsum("ac,jbc->jab", query, sources, preferred_element_type=jnp.float32)
    scale = jnp.sqrt(jnp.float32(query.shape[1]))
    return (inner / (scale * query_rms[None, :, None] * source_rms[:, None, :])).astype(
        jnp.bfloat16
    )


def per_device(
    query_maps, source_maps, hubs, pick, weight_first, bias_first, weight_second, bias_second
):
    owners = pick[0]
    cells, channels = source_maps.shape
    chosen = jnp.zeros((2, cells, channels), jnp.bfloat16)
    for index in range(HUBS):
        arrived = spread(source_maps, "wide", hubs[index])
        chosen = jnp.where((owners == index)[:, None, None], arrived[None], chosen)
    correlation = scaled_corr(query_maps, chosen)
    volumes = jnp.concatenate([correlation, jnp.swapaxes(correlation, 1, 2)], axis=0)

    def filter_one(matrix):
        return consensus_net(matrix, weight_first, bias_first, weight_second, bias_second)

    filtered = lax.map(filter_one, volumes)
    return (filtered[:2] + jnp.swapaxes(filtered[2:], 1, 2))[None]


def solution(mesh):
    return jax.shard_map(
        per_device,
        mesh=mesh,
        in_specs=(
            P(("grp", "wide"), None),
            P(("grp", "wide"), None),
            P("grp"),
            P(("grp", "wide"), None),
            P(),
            P(),
            P(),
            P(),
        ),
        out_specs=P(("grp", "wide"), None, None, None),
        check_vma=False,
    )
```

profile of v0, /device:TPU:0, one launch (start us, length us, event | category | flops | bytes accessed | tf_op | source)
XLA Modules:
  0.0 569.2 jit_solution(4240992218030931366)
XLA Ops:
  14.3 95.2 %all-reduce.5.cloned.1.call-done = (bf16[128,1024]{1,0:T(8,128)(2,1)}, bf16[128,1024]{1,0:T(8,128)(2,1)}, bf16[128,1024]{1,0:T(8,128)(2,1)}, bf16[128,1024]{1,0:T(8,128)(2,1)}) async-done(((bf16[128,1024]{1,0:T(8,128)(2,1)}, bf16[128,1024]{1,0:T(8,128)(2,1)}, bf16[128,1024]{1,0:T(8,128)(2,1)}, bf16[128,1024]{1,0:T(8,128)(2,1)}), (bf16[128,1024]{1,0:T(8,128)(2,1)}, bf16[128,1024]{1,0:T(8,128)(2,1)}, ...) | async-done | bytes 1048592 | tf_op jit(solution)/shard_map/psum | solution.py:13
  113.0 448.3 %while.12 = (s32[]{:T(128)}, f32[4,128,128]{2,1,0:T(8,128)S(1)}, bf16[4,128,128]{2,1,0:T(8,128)(2,1)S(1)}, bf16[16,1,3,3,3,3]{0,5,4,3,2,1:T(4,128)(2,1)S(1)}, f3...) while((s32[]{:T(128)}, f32[4,128,128]{2,1,0:T(8,128)S(1)}, ...), condition=%wide.region_7.8_spmd, body=%wide.region_6.7_spmd.sunk | while | flops 100311040 | bytes 41547692 | solution.py:70
  114.6 6.2 %fusion.91 = f32[32,4,32,5,16]{2,4,3,1,0:T(8,128)} fusion(bf16[1,32,4,32,7]{3,0,4,2,1:T(2,128)(2,1)S(1)} %copy.115, bf16[16,1,3,3,3]{0,4,3,2,1:T(4,128)(2,1)S(1)} %get-tuple-element.216), kind=kOutput, calls=%fused_computation.45.clone.1 | convolution fusion | flops 14438400 | bytes 1368928 | tf_op jit(solution)/shard_map/while/body/eval_jaxpr/conv_general_dilated | solution.py:21
  121.5 6.1 %fusion.89 = f32[32,4,32,5,16]{2,4,3,1,0:T(8,128)} fusion(bf16[1,32,4,32,7]{3,0,4,2,1:T(2,128)(2,1)S(1)} %copy.113, bf16[16,1,3,3,3]{0,4,3,2,1:T(4,128)(2,1)S(1)} %get-tuple-element.214), kind=kOutput, calls=%fused_computation.43.clone.1 | convolution fusion | flops 14438400 | bytes 1368928 | tf_op jit(solution)/shard_map/while/body/eval_jaxpr/conv_general_dilated | solution.py:21
  128.3 9.4 %broadcast_select_fusion.6 = (bf16[32,4,32,5,16]{2,4,3,1,0:T(8,128)(2,1)}, bf16[32,4,32,5,16]{2,4,3,1,0:T(8,128)(2,1)}) fusion(pred[32,5]{0,1:T(8,128)(4,1)S(1)} %get-tuple-element.254, f32[16]{0:T(128)S(1)} %get-tuple-element.250, bf16[1,32,4,32,7]{3,0,4,2,1:T(2,128)(2,1)S(1)} %copy.111, bf16[16,1,3,3,3]{0,4,3,2,1:T(4,128)(2,1)S(1)} %get-tuple-element.213, ...), kind=kOutput, calls=%fused_computation.14.clone.1 | convolution fusion | flops 17387520 | bytes 3990592 | tf_op jit(solution)/shard_map/while/body/eval_jaxpr/conv_general_dilated | solution.py:21
  137.7 5.1 copy.116
  148.1 10.4 %copy.120 = bf16[16,32,4,32,7]{3,0,4,2,1:T(8,128)(2,1)} copy(bf16[16,32,4,32,7]{1,0,4,3,2:T(8,128)(2,1)} %bitcast.140) | data formatting | bytes 1835008 | tf_op jit(solution)/shard_map/while/body/eval_jaxpr/conv_general_dilated | solution.py:21
  158.5 4.9 copy.118
  166.0 10.6 %copy.119 = bf16[32,4,32,7,16]{2,4,3,1,0:T(8,128)(2,1)} copy(bf16[32,4,32,7,16]{0,4,3,2,1:T(8,128)(2,1)} %bitcast.139) | data formatting | bytes 1835008 | tf_op jit(solution)/shard_map/while/body/eval_jaxpr/convert_element_type | solution.py:36
  177.3 2.3 fusion.93
  179.6 10.4 %copy.117 = bf16[16,32,4,32,7]{3,0,4,2,1:T(8,128)(2,1)} copy(bf16[16,32,4,32,7]{1,0,4,3,2:T(8,128)(2,1)} %bitcast.141) | data formatting | bytes 1835008 | tf_op jit(solution)/shard_map/while/body/eval_jaxpr/conv_general_dilated | solution.py:21
  190.1 11.1 %convolution_select_fusion.3 = f32[32,4,32,5,1]{2,4,3,1,0:T(1,128)S(1)} fusion(bf16[16,32,4,32,7]{3,0,4,2,1:T(8,128)(2,1)} %copy.117, pred[32,5]{0,1:T(8,128)(4,1)S(1)} %get-tuple-element.254, bf16[1,16,3,3,3]{1,4,3,2,0:T(4,128)(2,1)S(1)} %get-tuple-element.219), kind=kOutput, calls=%fused_computation.23.clone.1 | convolution fusion | flops 14458880 | bytes 1000448 | tf_op jit(solution)/shard_map/while/body/eval_jaxpr/conv_general_dilated | solution.py:21
  201.1 8.9 %convolution_add_fusion.2 = f32[32,4,32,5,1]{2,4,3,1,0:T(1,128)S(1)} fusion(f32[32,4,32,5,1]{2,4,3,1,0:T(1,128)S(1)} %convolution_select_fusion.3, bf16[32,4,32,7,16]{2,4,3,1,0:T(8,128)(2,1)S(1)} %copy-done.2, bf16[1,16,3,3,3]{1,4,3,2,0:T(4,128)(2,1)S(1)} %get-tuple-element.223), kind=kOutput, calls=%fused_computation.18.clone.1 | convolution fusion | flops 14458880 | bytes 1082208 | tf_op jit(solution)/shard_map/while/body/eval_jaxpr/conv_general_dilated | solution.py:21
  210.1 10.0 %fusion.97 = f32[32,4,32,5,1]{2,4,3,1,0:T(1,128)S(1)} fusion(f32[32,4,32,5,1]{2,4,3,1,0:T(1,128)S(1)} %convolution_add_fusion.2, bf16[16,32,4,32,7]{3,0,4,2,1:T(8,128)(2,1)S(1)} %copy-done.1, pred[32,5]{0,1:T(8,128)(4,1)S(1)} %get-tuple-element.254, f32[]{:T(128)} %bitcast.137, bf16[1,16,3,3,3]{1,4,3,2,0:T(4,128)(2,1)S(1)} %get-tuple-element.225), kind=kOutput, calls=%fused_computation.22.clone.1 | convolution fusion | flops 14520320 | bytes 1082372 | tf_op jit(solution)/shard_map/while/body/eval_jaxpr/conv_general_dilated | solution.py:21
  226.3 6.2 %fusion.91 = f32[32,4,32,5,16]{2,4,3,1,0:T(8,128)} fusion(bf16[1,32,4,32,7]{3,0,4,2,1:T(2,128)(2,1)S(1)} %copy.115, bf16[16,1,3,3,3]{0,4,3,2,1:T(4,128)(2,1)S(1)} %get-tuple-element.216), kind=kOutput, calls=%fused_computation.45.clone.1 | convolution fusion | flops 14438400 | bytes 1368928 | tf_op jit(solution)/shard_map/while/body/eval_jaxpr/conv_general_dilated | solution.py:21
  233.2 6.1 %fusion.89 = f32[32,4,32,5,16]{2,4,3,1,0:T(8,128)} fusion(bf16[1,32,4,32,7]{3,0,4,2,1:T(2,128)(2,1)S(1)} %copy.113, bf16[16,1,3,3,3]{0,4,3,2,1:T(4,128)(2,1)S(1)} %get-tuple-element.214), kind=kOutput, calls=%fused_computation.43.clone.1 | convolution fusion | flops 14438400 | bytes 1368928 | tf_op jit(solution)/shard_map/while/body/eval_jaxpr/conv_general_dilated | solution.py:21
  240.0 9.4 %broadcast_select_fusion.6 = (bf16[32,4,32,5,16]{2,4,3,1,0:T(8,128)(2,1)}, bf16[32,4,32,5,16]{2,4,3,1,0:T(8,128)(2,1)}) fusion(pred[32,5]{0,1:T(8,128)(4,1)S(1)} %get-tuple-element.254, f32[16]{0:T(128)S(1)} %get-tuple-element.250, bf16[1,32,4,32,7]{3,0,4,2,1:T(2,128)(2,1)S(1)} %copy.111, bf16[16,1,3,3,3]{0,4,3,2,1:T(4,128)(2,1)S(1)} %get-tuple-element.213, ...), kind=kOutput, calls=%fused_computation.14.clone.1 | convolution fusion | flops 17387520 | bytes 3990592 | tf_op jit(solution)/shard_map/while/body/eval_jaxpr/conv_general_dilated | solution.py:21
  249.4 5.2 copy.116
  259.8 10.4 %copy.120 = bf16[16,32,4,32,7]{3,0,4,2,1:T(8,128)(2,1)} copy(bf16[16,32,4,32,7]{1,0,4,3,2:T(8,128)(2,1)} %bitcast.140) | data formatting | bytes 1835008 | tf_op jit(solution)/shard_map/while/body/eval_jaxpr/conv_general_dilated | solution.py:21
  270.2 4.9 copy.118
  277.7 10.6 %copy.119 = bf16[32,4,32,7,16]{2,4,3,1,0:T(8,128)(2,1)} copy(bf16[32,4,32,7,16]{0,4,3,2,1:T(8,128)(2,1)} %bitcast.139) | data formatting | bytes 1835008 | tf_op jit(solution)/shard_map/while/body/eval_jaxpr/convert_element_type | solution.py:36
  291.3 10.4 %copy.117 = bf16[16,32,4,32,7]{3,0,4,2,1:T(8,128)(2,1)} copy(bf16[16,32,4,32,7]{1,0,4,3,2:T(8,128)(2,1)} %bitcast.141) | data formatting | bytes 1835008 | tf_op jit(solution)/shard_map/while/body/eval_jaxpr/conv_general_dilated | solution.py:21
  301.8 11.2 %convolution_select_fusion.3 = f32[32,4,32,5,1]{2,4,3,1,0:T(1,128)S(1)} fusion(bf16[16,32,4,32,7]{3,0,4,2,1:T(8,128)(2,1)} %copy.117, pred[32,5]{0,1:T(8,128)(4,1)S(1)} %get-tuple-element.254, bf16[1,16,3,3,3]{1,4,3,2,0:T(4,128)(2,1)S(1)} %get-tuple-element.219), kind=kOutput, calls=%fused_computation.23.clone.1 | convolution fusion | flops 14458880 | bytes 1000448 | tf_op jit(solution)/shard_map/while/body/eval_jaxpr/conv_general_dilated | solution.py:21
  313.0 8.9 %convolution_add_fusion.2 = f32[32,4,32,5,1]{2,4,3,1,0:T(1,128)S(1)} fusion(f32[32,4,32,5,1]{2,4,3,1,0:T(1,128)S(1)} %convolution_select_fusion.3, bf16[32,4,32,7,16]{2,4,3,1,0:T(8,128)(2,1)S(1)} %copy-done.2, bf16[1,16,3,3,3]{1,4,3,2,0:T(4,128)(2,1)S(1)} %get-tuple-element.223), kind=kOutput, calls=%fused_computation.18.clone.1 | convolution fusion | flops 14458880 | bytes 1082208 | tf_op jit(solution)/shard_map/while/body/eval_jaxpr/conv_general_dilated | solution.py:21
  322.0 9.7 %fusion.97 = f32[32,4,32,5,1]{2,4,3,1,0:T(1,128)S(1)} fusion(f32[32,4,32,5,1]{2,4,3,1,0:T(1,128)S(1)} %convolution_add_fusion.2, bf16[16,32,4,32,7]{3,0,4,2,1:T(8,128)(2,1)S(1)} %copy-done.1, pred[32,5]{0,1:T(8,128)(4,1)S(1)} %get-tuple-element.254, f32[]{:T(128)} %bitcast.137, bf16[1,16,3,3,3]{1,4,3,2,0:T(4,128)(2,1)S(1)} %get-tuple-element.225), kind=kOutput, calls=%fused_computation.22.clone.1 | convolution fusion | flops 14520320 | bytes 1082372 | tf_op jit(solution)/shard_map/while/body/eval_jaxpr/conv_general_dilated | solution.py:21
  338.0 6.2 %fusion.91 = f32[32,4,32,5,16]{2,4,3,1,0:T(8,128)} fusion(bf16[1,32,4,32,7]{3,0,4,2,1:T(2,128)(2,1)S(1)} %copy.115, bf16[16,1,3,3,3]{0,4,3,2,1:T(4,128)(2,1)S(1)} %get-tuple-element.216), kind=kOutput, calls=%fused_computation.45.clone.1 | convolution fusion | flops 14438400 | bytes 1368928 | tf_op jit(solution)/shard_map/while/body/eval_jaxpr/conv_general_dilated | solution.py:21
  344.9 6.1 %fusion.89 = f32[32,4,32,5,16]{2,4,3,1,0:T(8,128)} fusion(bf16[1,32,4,32,7]{3,0,4,2,1:T(2,128)(2,1)S(1)} %copy.113, bf16[16,1,3,3,3]{0,4,3,2,1:T(4,128)(2,1)S(1)} %get-tuple-element.214), kind=kOutput, calls=%fused_computation.43.clone.1 | convolution fusion | flops 14438400 | bytes 1368928 | tf_op jit(solution)/shard_map/while/body/eval_jaxpr/conv_general_dilated | solution.py:21
  351.7 9.4 %broadcast_select_fusion.6 = (bf16[32,4,32,5,16]{2,4,3,1,0:T(8,128)(2,1)}, bf16[32,4,32,5,16]{2,4,3,1,0:T(8,128)(2,1)}) fusion(pred[32,5]{0,1:T(8,128)(4,1)S(1)} %get-tuple-element.254, f32[16]{0:T(128)S(1)} %get-tuple-element.250, bf16[1,32,4,32,7]{3,0,4,2,1:T(2,128)(2,1)S(1)} %copy.111, bf16[16,1,3,3,3]{0,4,3,2,1:T(4,128)(2,1)S(1)} %get-tuple-element.213, ...), kind=kOutput, calls=%fused_computation.14.clone.1 | convolution fusion | flops 17387520 | bytes 3990592 | tf_op jit(solution)/shard_map/while/body/eval_jaxpr/conv_general_dilated | solution.py:21
  361.1 5.3 copy.116
  371.7 10.4 %copy.120 = bf16[16,32,4,32,7]{3,0,4,2,1:T(8,128)(2,1)} copy(bf16[16,32,4,32,7]{1,0,4,3,2:T(8,128)(2,1)} %bitcast.140) | data formatting | bytes 1835008 | tf_op jit(solution)/shard_map/while/body/eval_jaxpr/conv_general_dilated | solution.py:21
  382.1 4.9 copy.118
  389.6 10.6 %copy.119 = bf16[32,4,32,7,16]{2,4,3,1,0:T(8,128)(2,1)} copy(bf16[32,4,32,7,16]{0,4,3,2,1:T(8,128)(2,1)} %bitcast.139) | data formatting | bytes 1835008 | tf_op jit(solution)/shard_map/while/body/eval_jaxpr/convert_element_type | solution.py:36
  400.9 2.3 fusion.93
  403.2 10.4 %copy.117 = bf16[16,32,4,32,7]{3,0,4,2,1:T(8,128)(2,1)} copy(bf16[16,32,4,32,7]{1,0,4,3,2:T(8,128)(2,1)} %bitcast.141) | data formatting | bytes 1835008 | tf_op jit(solution)/shard_map/while/body/eval_jaxpr/conv_general_dilated | solution.py:21
  413.7 11.0 %convolution_select_fusion.3 = f32[32,4,32,5,1]{2,4,3,1,0:T(1,128)S(1)} fusion(bf16[16,32,4,32,7]{3,0,4,2,1:T(8,128)(2,1)} %copy.117, pred[32,5]{0,1:T(8,128)(4,1)S(1)} %get-tuple-element.254, bf16[1,16,3,3,3]{1,4,3,2,0:T(4,128)(2,1)S(1)} %get-tuple-element.219), kind=kOutput, calls=%fused_computation.23.clone.1 | convolution fusion | flops 14458880 | bytes 1000448 | tf_op jit(solution)/shard_map/while/body/eval_jaxpr/conv_general_dilated | solution.py:21
  424.7 8.9 %convolution_add_fusion.2 = f32[32,4,32,5,1]{2,4,3,1,0:T(1,128)S(1)} fusion(f32[32,4,32,5,1]{2,4,3,1,0:T(1,128)S(1)} %convolution_select_fusion.3, bf16[32,4,32,7,16]{2,4,3,1,0:T(8,128)(2,1)S(1)} %copy-done.2, bf16[1,16,3,3,3]{1,4,3,2,0:T(4,128)(2,1)S(1)} %get-tuple-element.223), kind=kOutput, calls=%fused_computation.18.clone.1 | convolution fusion | flops 14458880 | bytes 1082208 | tf_op jit(solution)/shard_map/while/body/eval_jaxpr/conv_general_dilated | solution.py:21
  433.7 9.8 %fusion.97 = f32[32,4,32,5,1]{2,4,3,1,0:T(1,128)S(1)} fusion(f32[32,4,32,5,1]{2,4,3,1,0:T(1,128)S(1)} %convolution_add_fusion.2, bf16[16,32,4,32,7]{3,0,4,2,1:T(8,128)(2,1)S(1)} %copy-done.1, pred[32,5]{0,1:T(8,128)(4,1)S(1)} %get-tuple-element.254, f32[]{:T(128)} %bitcast.137, bf16[1,16,3,3,3]{1,4,3,2,0:T(4,128)(2,1)S(1)} %get-tuple-element.225), kind=kOutput, calls=%fused_computation.22.clone.1 | convolution fusion | flops 14520320 | bytes 1082372 | tf_op jit(solution)/shard_map/while/body/eval_jaxpr/conv_general_dilated | solution.py:21
  449.9 6.2 %fusion.91 = f32[32,4,32,5,16]{2,4,3,1,0:T(8,128)} fusion(bf16[1,32,4,32,7]{3,0,4,2,1:T(2,128)(2,1)S(1)} %copy.115, bf16[16,1,3,3,3]{0,4,3,2,1:T(4,128)(2,1)S(1)} %get-tuple-element.216), kind=kOutput, calls=%fused_computation.45.clone.1 | convolution fusion | flops 14438400 | bytes 1368928 | tf_op jit(solution)/shard_map/while/body/eval_jaxpr/conv_general_dilated | solution.py:21
  456.8 6.1 %fusion.89 = f32[32,4,32,5,16]{2,4,3,1,0:T(8,128)} fusion(bf16[1,32,4,32,7]{3,0,4,2,1:T(2,128)(2,1)S(1)} %copy.113, bf16[16,1,3,3,3]{0,4,3,2,1:T(4,128)(2,1)S(1)} %get-tuple-element.214), kind=kOutput, calls=%fused_computation.43.clone.1 | convolution fusion | flops 14438400 | bytes 1368928 | tf_op jit(solution)/shard_map/while/body/eval_jaxpr/conv_general_dilated | solution.py:21
  463.6 9.4 %broadcast_select_fusion.6 = (bf16[32,4,32,5,16]{2,4,3,1,0:T(8,128)(2,1)}, bf16[32,4,32,5,16]{2,4,3,1,0:T(8,128)(2,1)}) fusion(pred[32,5]{0,1:T(8,128)(4,1)S(1)} %get-tuple-element.254, f32[16]{0:T(128)S(1)} %get-tuple-element.250, bf16[1,32,4,32,7]{3,0,4,2,1:T(2,128)(2,1)S(1)} %copy.111, bf16[16,1,3,3,3]{0,4,3,2,1:T(4,128)(2,1)S(1)} %get-tuple-element.213, ...), kind=kOutput, calls=%fused_computation.14.clone.1 | convolution fusion | flops 17387520 | bytes 3990592 | tf_op jit(solution)/shard_map/while/body/eval_jaxpr/conv_general_dilated | solution.py:21
  473.0 5.1 copy.116
  483.4 10.4 %copy.120 = bf16[16,32,4,32,7]{3,0,4,2,1:T(8,128)(2,1)} copy(bf16[16,32,4,32,7]{1,0,4,3,2:T(8,128)(2,1)} %bitcast.140) | data formatting | bytes 1835008 | tf_op jit(solution)/shard_map/while/body/eval_jaxpr/conv_general_dilated | solution.py:21
  493.8 4.9 copy.118
  501.2 10.6 %copy.119 = bf16[32,4,32,7,16]{2,4,3,1,0:T(8,128)(2,1)} copy(bf16[32,4,32,7,16]{0,4,3,2,1:T(8,128)(2,1)} %bitcast.139) | data formatting | bytes 1835008 | tf_op jit(solution)/shard_map/while/body/eval_jaxpr/convert_element_type | solution.py:36
  514.9 10.4 %copy.117 = bf16[16,32,4,32,7]{3,0,4,2,1:T(8,128)(2,1)} copy(bf16[16,32,4,32,7]{1,0,4,3,2:T(8,128)(2,1)} %bitcast.141) | data formatting | bytes 1835008 | tf_op jit(solution)/shard_map/while/body/eval_jaxpr/conv_general_dilated | solution.py:21
  525.3 11.1 %convolution_select_fusion.3 = f32[32,4,32,5,1]{2,4,3,1,0:T(1,128)S(1)} fusion(bf16[16,32,4,32,7]{3,0,4,2,1:T(8,128)(2,1)} %copy.117, pred[32,5]{0,1:T(8,128)(4,1)S(1)} %get-tuple-element.254, bf16[1,16,3,3,3]{1,4,3,2,0:T(4,128)(2,1)S(1)} %get-tuple-element.219), kind=kOutput, calls=%fused_computation.23.clone.1 | convolution fusion | flops 14458880 | bytes 1000448 | tf_op jit(solution)/shard_map/while/body/eval_jaxpr/conv_general_dilated | solution.py:21
  536.4 8.9 %convolution_add_fusion.2 = f32[32,4,32,5,1]{2,4,3,1,0:T(1,128)S(1)} fusion(f32[32,4,32,5,1]{2,4,3,1,0:T(1,128)S(1)} %convolution_select_fusion.3, bf16[32,4,32,7,16]{2,4,3,1,0:T(8,128)(2,1)S(1)} %copy-done.2, bf16[1,16,3,3,3]{1,4,3,2,0:T(4,128)(2,1)S(1)} %get-tuple-element.223), kind=kOutput, calls=%fused_computation.18.clone.1 | convolution fusion | flops 14458880 | bytes 1082208 | tf_op jit(solution)/shard_map/while/body/eval_jaxpr/conv_general_dilated | solution.py:21
  545.4 10.0 %fusion.97 = f32[32,4,32,5,1]{2,4,3,1,0:T(1,128)S(1)} fusion(f32[32,4,32,5,1]{2,4,3,1,0:T(1,128)S(1)} %convolution_add_fusion.2, bf16[16,32,4,32,7]{3,0,4,2,1:T(8,128)(2,1)S(1)} %copy-done.1, pred[32,5]{0,1:T(8,128)(4,1)S(1)} %get-tuple-element.254, f32[]{:T(128)} %bitcast.137, bf16[1,16,3,3,3]{1,4,3,2,0:T(4,128)(2,1)S(1)} %get-tuple-element.225), kind=kOutput, calls=%fused_computation.22.clone.1 | convolution fusion | flops 14520320 | bytes 1082372 | tf_op jit(solution)/shard_map/while/body/eval_jaxpr/conv_general_dilated | solution.py:21
  (192 shorter events, 61.4 us)
Async XLA Ops:
  6.5 104.6 %copy-start.5 = (bf16[128,1024]{1,0:T(8,128)(2,1)S(1)}, bf16[128,1024]{1,0:T(8,128)(2,1)}, u32[]{:S(2)}) copy-start(bf16[128,1024]{1,0:T(8,128)(2,1)} %param.10) | copy-start | bytes 786436
  6.5 103.0 %all-reduce.5.cloned.1.call-start = ((), (), s32[]{:S(2)}) async-start(), calls=%async_computation | async-start | bytes 2097152 | tf_op jit(solution)/shard_map/psum | solution.py:13
  10.4 102.5 %copy-start.3 = (bf16[16,1,3,3,3,3]{0,5,4,3,2,1:T(4,128)(2,1)S(1)}, bf16[16,1,3,3,3,3]{0,5,4,3,2,1:T(4,128)(2,1)}, u32[]{:S(2)}) copy-start(bf16[16,1,3,3,3,3]{0,5,4,3,2,1:T(4,128)(2,1)} %param.14) | copy-start | bytes 7780
  10.5 102.5 %copy-start.4 = (bf16[1,16,3,3,3,3]{1,5,4,3,2,0:T(4,128)(2,1)S(1)}, bf16[1,16,3,3,3,3]{1,5,4,3,2,0:T(4,128)(2,1)}, u32[]{:S(2)}) copy-start(bf16[1,16,3,3,3,3]{1,5,4,3,2,0:T(4,128)(2,1)} %param.16) | copy-start | bytes 7780
  10.5 102.5 %copy-start.6 = (f32[16]{0:T(128)S(1)}, f32[16]{0:T(128)}, u32[]{:S(2)}) copy-start(f32[16]{0:T(128)} %param.15) | copy-start | bytes 196
  10.5 102.5 %copy-start.7 = (pred[32,5]{0,1:T(8,128)(4,1)S(1)}, pred[32,5]{0,1:T(8,128)(4,1)}, u32[]{:S(2)}) copy-start(pred[32,5]{0,1:T(8,128)(4,1)} %constant.157) | copy-start | bytes 484
  166.0 10.6 %copy-start = (bf16[16,32,4,4,32]{1,0,4,3,2:T(8,128)(2,1)S(1)}, bf16[16,32,4,4,32]{1,0,4,3,2:T(8,128)(2,1)}, u32[]{:S(2)}) copy-start(bf16[16,32,4,4,32]{1,0,4,3,2:T(8,128)(2,1)} %get-tuple-element.218) | copy-start | bytes 1572868 | tf_op jit(solution)/shard_map/while
  190.0 11.1 %copy-start.2 = (bf16[32,4,32,7,16]{2,4,3,1,0:T(8,128)(2,1)S(1)}, bf16[32,4,32,7,16]{2,4,3,1,0:T(8,128)(2,1)}, u32[]{:S(2)}) copy-start(bf16[32,4,32,7,16]{2,4,3,1,0:T(8,128)(2,1)} %copy.119) | copy-start | bytes 2752516 | tf_op jit(solution)/shard_map/while
  201.1 9.0 %copy-start.1 = (bf16[16,32,4,32,7]{3,0,4,2,1:T(8,128)(2,1)S(1)}, bf16[16,32,4,32,7]{3,0,4,2,1:T(8,128)(2,1)}, u32[]{:S(2)}) copy-start(bf16[16,32,4,32,7]{3,0,4,2,1:T(8,128)(2,1)} %copy.120) | copy-start | bytes 2752516 | tf_op jit(solution)/shard_map/while
  277.7 10.6 %copy-start = (bf16[16,32,4,4,32]{1,0,4,3,2:T(8,128)(2,1)S(1)}, bf16[16,32,4,4,32]{1,0,4,3,2:T(8,128)(2,1)}, u32[]{:S(2)}) copy-start(bf16[16,32,4,4,32]{1,0,4,3,2:T(8,128)(2,1)} %get-tuple-element.218) | copy-start | bytes 1572868 | tf_op jit(solution)/shard_map/while
  301.7 11.3 %copy-start.2 = (bf16[32,4,32,7,16]{2,4,3,1,0:T(8,128)(2,1)S(1)}, bf16[32,4,32,7,16]{2,4,3,1,0:T(8,128)(2,1)}, u32[]{:S(2)}) copy-start(bf16[32,4,32,7,16]{2,4,3,1,0:T(8,128)(2,1)} %copy.119) | copy-start | bytes 2752516 | tf_op jit(solution)/shard_map/while
  313.0 9.0 %copy-start.1 = (bf16[16,32,4,32,7]{3,0,4,2,1:T(8,128)(2,1)S(1)}, bf16[16,32,4,32,7]{3,0,4,2,1:T(8,128)(2,1)}, u32[]{:S(2)}) copy-start(bf16[16,32,4,32,7]{3,0,4,2,1:T(8,128)(2,1)} %copy.120) | copy-start | bytes 2752516 | tf_op jit(solution)/shard_map/while
  389.6 10.6 %copy-start = (bf16[16,32,4,4,32]{1,0,4,3,2:T(8,128)(2,1)S(1)}, bf16[16,32,4,4,32]{1,0,4,3,2:T(8,128)(2,1)}, u32[]{:S(2)}) copy-start(bf16[16,32,4,4,32]{1,0,4,3,2:T(8,128)(2,1)} %get-tuple-element.218) | copy-start | bytes 1572868 | tf_op jit(solution)/shard_map/while
  413.6 11.0 %copy-start.2 = (bf16[32,4,32,7,16]{2,4,3,1,0:T(8,128)(2,1)S(1)}, bf16[32,4,32,7,16]{2,4,3,1,0:T(8,128)(2,1)}, u32[]{:S(2)}) copy-start(bf16[32,4,32,7,16]{2,4,3,1,0:T(8,128)(2,1)} %copy.119) | copy-start | bytes 2752516 | tf_op jit(solution)/shard_map/while
  424.7 9.0 %copy-start.1 = (bf16[16,32,4,32,7]{3,0,4,2,1:T(8,128)(2,1)S(1)}, bf16[16,32,4,32,7]{3,0,4,2,1:T(8,128)(2,1)}, u32[]{:S(2)}) copy-start(bf16[16,32,4,32,7]{3,0,4,2,1:T(8,128)(2,1)} %copy.120) | copy-start | bytes 2752516 | tf_op jit(solution)/shard_map/while
  501.2 10.6 %copy-start = (bf16[16,32,4,4,32]{1,0,4,3,2:T(8,128)(2,1)S(1)}, bf16[16,32,4,4,32]{1,0,4,3,2:T(8,128)(2,1)}, u32[]{:S(2)}) copy-start(bf16[16,32,4,4,32]{1,0,4,3,2:T(8,128)(2,1)} %get-tuple-element.218) | copy-start | bytes 1572868 | tf_op jit(solution)/shard_map/while
  525.3 11.1 %copy-start.2 = (bf16[32,4,32,7,16]{2,4,3,1,0:T(8,128)(2,1)S(1)}, bf16[32,4,32,7,16]{2,4,3,1,0:T(8,128)(2,1)}, u32[]{:S(2)}) copy-start(bf16[32,4,32,7,16]{2,4,3,1,0:T(8,128)(2,1)} %copy.119) | copy-start | bytes 2752516 | tf_op jit(solution)/shard_map/while
  536.4 9.0 %copy-start.1 = (bf16[16,32,4,32,7]{3,0,4,2,1:T(8,128)(2,1)S(1)}, bf16[16,32,4,32,7]{3,0,4,2,1:T(8,128)(2,1)}, u32[]{:S(2)}) copy-start(bf16[16,32,4,32,7]{3,0,4,2,1:T(8,128)(2,1)} %copy.120) | copy-start | bytes 2752516 | tf_op jit(solution)/shard_map/while
Sparse Core Ops, SparseCore 0:
  12.6 96.8 all-reduce.4
where the time goes:
time: 572 us; the launch traced here: 569 us
  matrix products  208 us (36%)
  local copies, waits for them, and re-layouts  195 us (34%)
  waiting for transfers between devices  95.2 us (17%)
  other arithmetic  35.3 us (6%)
  loops' own time  19.6 us (3%)
  between operations  16.2 us (3%)
    conv_general_dilated x24, matrix products, conv_volume(): lax.conv_general_dilated(padded[offset:offset + height], kernel[:, :, off...  206 us
    psum x1, waiting for transfers between devices, spread(): return lax.psum(kept, axis)  95.2 us
    conv_general_dilated x52, local copies, waits for them, and re-layouts, conv_volume(): lax.conv_general_dilated(padded[offset:offset + height], kernel[:, :, off...  89.9 us
    convert_element_type x20, local copies, waits for them, and re-layouts, consensus_net(): hidden = jax.nn.relu(preact).astype(jnp.bfloat16)  85.1 us
    conv_general_dilated x20, other arithmetic, conv_volume(): lax.conv_general_dilated(padded[offset:offset + height], kernel[:, :, off...  19.8 us
    another operation x1, loops' own time, per_device(): filtered = lax.map(filter_one, volumes)  19.6 us
    slice x24, local copies, waits for them, and re-layouts, conv_volume(): padded[offset:offset + height]  13.8 us
  transfers between devices with their start and end apart: 1, of which 1 were waited for; matrix products, arithmetic and copies ran while one was open for 0% of the time, Pallas kernels for 0%

commit v1 on v0

--- a/solution.py
+++ b/solution.py
@@ -10,7 +10,11 @@
 
 def spread(value, axis, source):
     kept = jnp.where(lax.axis_index(axis) == source, value, 0).astype(value.dtype)
-    return lax.psum(kept, axis)
+
+    def arrange_the_lane(x_local):
+        return jax.lax.all_gather(x_local, axis_name=axis).sum(axis=0)
+
+    return arrange_the_lane(kept)
 
 
 def conv_volume(volume, kernel):

time: 572 us -> 685 us (1.20)
  waiting for transfers between devices: 95.2 us -> 195 us
  other arithmetic: 35.3 us -> 46.6 us
    all_gather x0 -> x4, waiting for transfers between devices: none -> 193 us  [arrange_the_lane(): return jax.lax.all_gather(x_local, axis_name=axis).sum(axis=0)]
    psum x1 -> x0, waiting for transfers between devices: 95.2 us -> none  [spread(): return lax.psum(kept, axis)]
    reduce_sum x0 -> x4, other arithmetic: none -> 12.5 us  [arrange_the_lane(): return jax.lax.all_gather(x_local, axis_name=axis).sum(axis=0)]
  transfers between devices with their start and end apart: 1 -> 4, of which waited for: 1 -> 4; matrix products, arithmetic and copies ran while one was open for 0% -> 2% of each run, Pallas kernels for 0% -> 0%
where the time goes in v1:
time: 685 us; the launch traced here: 679 us
  matrix products  206 us (30%)
  local copies, waits for them, and re-layouts  195 us (28%)
  waiting for transfers between devices  195 us (28%)
  other arithmetic  46.6 us (7%)
  loops' own time  19.6 us (3%)
  between operations  15.9 us (2%)
    conv_general_dilated x24, matrix products, conv_volume(): lax.conv_general_dilated(padded[offset:offset + height], kernel[:, :, off...  206 us
    all_gather x4, waiting for transfers between devices, arrange_the_lane(): return jax.lax.all_gather(x_local, axis_name=axis).sum(axis=0)  193 us
    conv_general_dilated x52, local copies, waits for them, and re-layouts, conv_volume(): lax.conv_general_dilated(padded[offset:offset + height], kernel[:, :, off...  89.9 us
    convert_element_type x20, local copies, waits for them, and re-layouts, consensus_net(): hidden = jax.nn.relu(preact).astype(jnp.bfloat16)  84.9 us
    conv_general_dilated x20, other arithmetic, conv_volume(): lax.conv_general_dilated(padded[offset:offset + height], kernel[:, :, off...  19.8 us
    another operation x1, loops' own time, per_device(): filtered = lax.map(filter_one, volumes)  19.6 us
    slice x24, local copies, waits for them, and re-layouts, conv_volume(): padded[offset:offset + height]  13.7 us
  transfers between devices with their start and end apart: 4, of which 4 were waited for; matrix products, arithmetic and copies ran while one was open for 2% of the time, Pallas kernels for 0%

profile of v1, /device:TPU:0, one launch (start us, length us, event | category | flops | bytes accessed | tf_op | source)
XLA Modules:
  0.0 678.9 jit_solution(17999909194057483840)
XLA Ops:
  16.3 49.4 %all-gather.9.cloned.1.call-done = bf16[2048,1024]{1,0:T(8,128)(2,1)} async-done(((bf16[128,1024]{1,0:T(8,128)(2,1)}), bf16[2048,1024]{1,0:T(8,128)(2,1)}) %all-gather.9.cloned.1.call-update) | async-done | bytes 4194320 | tf_op jit(solution)/shard_map/all_gather | solution.py:15
  68.8 48.0 %all-gather.11.cloned.1.call-done = bf16[2048,1024]{1,0:T(8,128)(2,1)} async-done(((bf16[128,1024]{1,0:T(8,128)(2,1)}), bf16[2048,1024]{1,0:T(8,128)(2,1)}) %all-gather.11.cloned.1.call-update) | async-done | bytes 4194320 | tf_op jit(solution)/shard_map/all_gather | solution.py:15
  119.9 48.0 %all-gather.13.cloned.1.call-done = bf16[2048,1024]{1,0:T(8,128)(2,1)} async-done(((bf16[128,1024]{1,0:T(8,128)(2,1)}), bf16[2048,1024]{1,0:T(8,128)(2,1)}) %all-gather.13.cloned.1.call-update) | async-done | bytes 4194320 | tf_op jit(solution)/shard_map/all_gather | solution.py:15
  171.0 47.8 %all-gather.15.cloned.1.call-done = bf16[2048,1024]{1,0:T(8,128)(2,1)} async-done(((bf16[128,1024]{1,0:T(8,128)(2,1)}), bf16[2048,1024]{1,0:T(8,128)(2,1)}) %all-gather.15.cloned.1.call-update) | async-done | bytes 4194320 | tf_op jit(solution)/shard_map/all_gather | solution.py:15
  223.1 448.2 %while.12 = (s32[]{:T(128)}, f32[4,128,128]{2,1,0:T(8,128)S(1)}, bf16[4,128,128]{2,1,0:T(8,128)(2,1)S(1)}, bf16[16,1,3,3,3,3]{0,5,4,3,2,1:T(4,128)(2,1)S(1)}, f3...) while((s32[]{:T(128)}, f32[4,128,128]{2,1,0:T(8,128)S(1)}, ...), condition=%wide.region_7.8_spmd, body=%wide.region_6.7_spmd.sunk | while | flops 100311040 | bytes 41547692 | solution.py:74
  224.8 6.2 fusion.91
  231.6 6.1 fusion.89
  238.4 9.4 %broadcast_select_fusion.6 = (bf16[32,4,32,5,16]{2,4,3,1,0:T(8,128)(2,1)}, bf16[32,4,32,5,16]{2,4,3,1,0:T(8,128)(2,1)}) fusion(pred[32,5]{0,1:T(8,128)(4,1)S(1)} %get-tuple-element.250, f32[16]{0:T(128)S(1)} %get-tuple-element.246, bf16[1,32,4,32,7]{3,0,4,2,1:T(2,128)(2,1)S(1)} %copy.111, bf16[16,1,3,3,3]{0,4,3,2,1:T(4,128)(2,1)S(1)} %get-tuple-element.209, ...), kind=kOutput, calls=%fused_computation.14.clone.1 | convolution fusion | flops 17387520 | bytes 3990592 | tf_op jit(solution)/shard_map/while/body/eval_jaxpr/conv_general_dilated | solution.py:25
  247.8 5.1 copy.116
  258.2 10.4 %copy.120 = bf16[16,32,4,32,7]{3,0,4,2,1:T(8,128)(2,1)} copy(bf16[16,32,4,32,7]{1,0,4,3,2:T(8,128)(2,1)} %bitcast.144) | data formatting | bytes 1835008 | tf_op jit(solution)/shard_map/while/body/eval_jaxpr/conv_general_dilated | solution.py:25
  268.6 4.9 copy.118
  276.1 10.5 %copy.119 = bf16[32,4,32,7,16]{2,4,3,1,0:T(8,128)(2,1)} copy(bf16[32,4,32,7,16]{0,4,3,2,1:T(8,128)(2,1)} %bitcast.143) | data formatting | bytes 1835008 | tf_op jit(solution)/shard_map/while/body/eval_jaxpr/convert_element_type | solution.py:40
  289.7 10.4 %copy.117 = bf16[16,32,4,32,7]{3,0,4,2,1:T(8,128)(2,1)} copy(bf16[16,32,4,32,7]{1,0,4,3,2:T(8,128)(2,1)} %bitcast.145) | data formatting | bytes 1835008 | tf_op jit(solution)/shard_map/while/body/eval_jaxpr/conv_general_dilated | solution.py:25
  300.1 11.1 %convolution_select_fusion.3 = f32[32,4,32,5,1]{2,4,3,1,0:T(1,128)S(1)} fusion(bf16[16,32,4,32,7]{3,0,4,2,1:T(8,128)(2,1)} %copy.117, pred[32,5]{0,1:T(8,128)(4,1)S(1)} %get-tuple-element.250, bf16[1,16,3,3,3]{1,4,3,2,0:T(4,128)(2,1)S(1)} %get-tuple-element.215), kind=kOutput, calls=%fused_computation.23.clone.1 | convolution fusion | flops 14458880 | bytes 1000448 | tf_op jit(solution)/shard_map/while/body/eval_jaxpr/conv_general_dilated | solution.py:25
  311.2 8.9 %convolution_add_fusion.2 = f32[32,4,32,5,1]{2,4,3,1,0:T(1,128)S(1)} fusion(f32[32,4,32,5,1]{2,4,3,1,0:T(1,128)S(1)} %convolution_select_fusion.3, bf16[32,4,32,7,16]{2,4,3,1,0:T(8,128)(2,1)S(1)} %copy-done.2, bf16[1,16,3,3,3]{1,4,3,2,0:T(4,128)(2,1)S(1)} %get-tuple-element.219), kind=kOutput, calls=%fused_computation.18.clone.1 | convolution fusion | flops 14458880 | bytes 1082208 | tf_op jit(solution)/shard_map/while/body/eval_jaxpr/conv_general_dilated | solution.py:25
  320.2 10.0 %fusion.97 = f32[32,4,32,5,1]{2,4,3,1,0:T(1,128)S(1)} fusion(f32[32,4,32,5,1]{2,4,3,1,0:T(1,128)S(1)} %convolution_add_fusion.2, bf16[16,32,4,32,7]{3,0,4,2,1:T(8,128)(2,1)S(1)} %copy-done.1, pred[32,5]{0,1:T(8,128)(4,1)S(1)} %get-tuple-element.250, f32[]{:T(128)} %bitcast.141, bf16[1,16,3,3,3]{1,4,3,2,0:T(4,128)(2,1)S(1)} %get-tuple-element.221), kind=kOutput, calls=%fused_computation.22.clone.1 | convolution fusion | flops 14520320 | bytes 1082372 | tf_op jit(solution)/shard_map/while/body/eval_jaxpr/conv_general_dilated | solution.py:25
  336.4 6.2 fusion.91
  343.2 6.1 fusion.89
  350.1 9.4 %broadcast_select_fusion.6 = (bf16[32,4,32,5,16]{2,4,3,1,0:T(8,128)(2,1)}, bf16[32,4,32,5,16]{2,4,3,1,0:T(8,128)(2,1)}) fusion(pred[32,5]{0,1:T(8,128)(4,1)S(1)} %get-tuple-element.250, f32[16]{0:T(128)S(1)} %get-tuple-element.246, bf16[1,32,4,32,7]{3,0,4,2,1:T(2,128)(2,1)S(1)} %copy.111, bf16[16,1,3,3,3]{0,4,3,2,1:T(4,128)(2,1)S(1)} %get-tuple-element.209, ...), kind=kOutput, calls=%fused_computation.14.clone.1 | convolution fusion | flops 17387520 | bytes 3990592 | tf_op jit(solution)/shard_map/while/body/eval_jaxpr/conv_general_dilated | solution.py:25
  359.4 5.2 copy.116
  369.9 10.4 %copy.120 = bf16[16,32,4,32,7]{3,0,4,2,1:T(8,128)(2,1)} copy(bf16[16,32,4,32,7]{1,0,4,3,2:T(8,128)(2,1)} %bitcast.144) | data formatting | bytes 1835008 | tf_op jit(solution)/shard_map/while/body/eval_jaxpr/conv_general_dilated | solution.py:25
  380.3 4.9 copy.118
  387.7 10.5 %copy.119 = bf16[32,4,32,7,16]{2,4,3,1,0:T(8,128)(2,1)} copy(bf16[32,4,32,7,16]{0,4,3,2,1:T(8,128)(2,1)} %bitcast.143) | data formatting | bytes 1835008 | tf_op jit(solution)/shard_map/while/body/eval_jaxpr/convert_element_type | solution.py:40
  401.4 10.4 %copy.117 = bf16[16,32,4,32,7]{3,0,4,2,1:T(8,128)(2,1)} copy(bf16[16,32,4,32,7]{1,0,4,3,2:T(8,128)(2,1)} %bitcast.145) | data formatting | bytes 1835008 | tf_op jit(solution)/shard_map/while/body/eval_jaxpr/conv_general_dilated | solution.py:25
  411.8 11.2 %convolution_select_fusion.3 = f32[32,4,32,5,1]{2,4,3,1,0:T(1,128)S(1)} fusion(bf16[16,32,4,32,7]{3,0,4,2,1:T(8,128)(2,1)} %copy.117, pred[32,5]{0,1:T(8,128)(4,1)S(1)} %get-tuple-element.250, bf16[1,16,3,3,3]{1,4,3,2,0:T(4,128)(2,1)S(1)} %get-tuple-element.215), kind=kOutput, calls=%fused_computation.23.clone.1 | convolution fusion | flops 14458880 | bytes 1000448 | tf_op jit(solution)/shard_map/while/body/eval_jaxpr/conv_general_dilated | solution.py:25
  423.1 8.9 %convolution_add_fusion.2 = f32[32,4,32,5,1]{2,4,3,1,0:T(1,128)S(1)} fusion(f32[32,4,32,5,1]{2,4,3,1,0:T(1,128)S(1)} %convolution_select_fusion.3, bf16[32,4,32,7,16]{2,4,3,1,0:T(8,128)(2,1)S(1)} %copy-done.2, bf16[1,16,3,3,3]{1,4,3,2,0:T(4,128)(2,1)S(1)} %get-tuple-element.219), kind=kOutput, calls=%fused_computation.18.clone.1 | convolution fusion | flops 14458880 | bytes 1082208 | tf_op jit(solution)/shard_map/while/body/eval_jaxpr/conv_general_dilated | solution.py:25
  432.0 9.7 %fusion.97 = f32[32,4,32,5,1]{2,4,3,1,0:T(1,128)S(1)} fusion(f32[32,4,32,5,1]{2,4,3,1,0:T(1,128)S(1)} %convolution_add_fusion.2, bf16[16,32,4,32,7]{3,0,4,2,1:T(8,128)(2,1)S(1)} %copy-done.1, pred[32,5]{0,1:T(8,128)(4,1)S(1)} %get-tuple-element.250, f32[]{:T(128)} %bitcast.141, bf16[1,16,3,3,3]{1,4,3,2,0:T(4,128)(2,1)S(1)} %get-tuple-element.221), kind=kOutput, calls=%fused_computation.22.clone.1 | convolution fusion | flops 14520320 | bytes 1082372 | tf_op jit(solution)/shard_map/while/body/eval_jaxpr/conv_general_dilated | solution.py:25
  448.1 6.2 fusion.91
  454.9 6.1 fusion.89
  461.7 9.4 %broadcast_select_fusion.6 = (bf16[32,4,32,5,16]{2,4,3,1,0:T(8,128)(2,1)}, bf16[32,4,32,5,16]{2,4,3,1,0:T(8,128)(2,1)}) fusion(pred[32,5]{0,1:T(8,128)(4,1)S(1)} %get-tuple-element.250, f32[16]{0:T(128)S(1)} %get-tuple-element.246, bf16[1,32,4,32,7]{3,0,4,2,1:T(2,128)(2,1)S(1)} %copy.111, bf16[16,1,3,3,3]{0,4,3,2,1:T(4,128)(2,1)S(1)} %get-tuple-element.209, ...), kind=kOutput, calls=%fused_computation.14.clone.1 | convolution fusion | flops 17387520 | bytes 3990592 | tf_op jit(solution)/shard_map/while/body/eval_jaxpr/conv_general_dilated | solution.py:25
  471.1 5.3 copy.116
  481.7 10.4 %copy.120 = bf16[16,32,4,32,7]{3,0,4,2,1:T(8,128)(2,1)} copy(bf16[16,32,4,32,7]{1,0,4,3,2:T(8,128)(2,1)} %bitcast.144) | data formatting | bytes 1835008 | tf_op jit(solution)/shard_map/while/body/eval_jaxpr/conv_general_dilated | solution.py:25
  492.1 4.9 copy.118
  499.6 10.5 %copy.119 = bf16[32,4,32,7,16]{2,4,3,1,0:T(8,128)(2,1)} copy(bf16[32,4,32,7,16]{0,4,3,2,1:T(8,128)(2,1)} %bitcast.143) | data formatting | bytes 1835008 | tf_op jit(solution)/shard_map/while/body/eval_jaxpr/convert_element_type | solution.py:40
  513.2 10.4 %copy.117 = bf16[16,32,4,32,7]{3,0,4,2,1:T(8,128)(2,1)} copy(bf16[16,32,4,32,7]{1,0,4,3,2:T(8,128)(2,1)} %bitcast.145) | data formatting | bytes 1835008 | tf_op jit(solution)/shard_map/while/body/eval_jaxpr/conv_general_dilated | solution.py:25
  523.6 11.0 %convolution_select_fusion.3 = f32[32,4,32,5,1]{2,4,3,1,0:T(1,128)S(1)} fusion(bf16[16,32,4,32,7]{3,0,4,2,1:T(8,128)(2,1)} %copy.117, pred[32,5]{0,1:T(8,128)(4,1)S(1)} %get-tuple-element.250, bf16[1,16,3,3,3]{1,4,3,2,0:T(4,128)(2,1)S(1)} %get-tuple-element.215), kind=kOutput, calls=%fused_computation.23.clone.1 | convolution fusion | flops 14458880 | bytes 1000448 | tf_op jit(solution)/shard_map/while/body/eval_jaxpr/conv_general_dilated | solution.py:25
  534.7 8.9 %convolution_add_fusion.2 = f32[32,4,32,5,1]{2,4,3,1,0:T(1,128)S(1)} fusion(f32[32,4,32,5,1]{2,4,3,1,0:T(1,128)S(1)} %convolution_select_fusion.3, bf16[32,4,32,7,16]{2,4,3,1,0:T(8,128)(2,1)S(1)} %copy-done.2, bf16[1,16,3,3,3]{1,4,3,2,0:T(4,128)(2,1)S(1)} %get-tuple-element.219), kind=kOutput, calls=%fused_computation.18.clone.1 | convolution fusion | flops 14458880 | bytes 1082208 | tf_op jit(solution)/shard_map/while/body/eval_jaxpr/conv_general_dilated | solution.py:25
  543.6 9.8 %fusion.97 = f32[32,4,32,5,1]{2,4,3,1,0:T(1,128)S(1)} fusion(f32[32,4,32,5,1]{2,4,3,1,0:T(1,128)S(1)} %convolution_add_fusion.2, bf16[16,32,4,32,7]{3,0,4,2,1:T(8,128)(2,1)S(1)} %copy-done.1, pred[32,5]{0,1:T(8,128)(4,1)S(1)} %get-tuple-element.250, f32[]{:T(128)} %bitcast.141, bf16[1,16,3,3,3]{1,4,3,2,0:T(4,128)(2,1)S(1)} %get-tuple-element.221), kind=kOutput, calls=%fused_computation.22.clone.1 | convolution fusion | flops 14520320 | bytes 1082372 | tf_op jit(solution)/shard_map/while/body/eval_jaxpr/conv_general_dilated | solution.py:25
  559.9 6.2 fusion.91
  566.8 6.1 fusion.89
  573.6 9.4 %broadcast_select_fusion.6 = (bf16[32,4,32,5,16]{2,4,3,1,0:T(8,128)(2,1)}, bf16[32,4,32,5,16]{2,4,3,1,0:T(8,128)(2,1)}) fusion(pred[32,5]{0,1:T(8,128)(4,1)S(1)} %get-tuple-element.250, f32[16]{0:T(128)S(1)} %get-tuple-element.246, bf16[1,32,4,32,7]{3,0,4,2,1:T(2,128)(2,1)S(1)} %copy.111, bf16[16,1,3,3,3]{0,4,3,2,1:T(4,128)(2,1)S(1)} %get-tuple-element.209, ...), kind=kOutput, calls=%fused_computation.14.clone.1 | convolution fusion | flops 17387520 | bytes 3990592 | tf_op jit(solution)/shard_map/while/body/eval_jaxpr/conv_general_dilated | solution.py:25
  582.9 5.1 copy.116
  593.3 10.4 %copy.120 = bf16[16,32,4,32,7]{3,0,4,2,1:T(8,128)(2,1)} copy(bf16[16,32,4,32,7]{1,0,4,3,2:T(8,128)(2,1)} %bitcast.144) | data formatting | bytes 1835008 | tf_op jit(solution)/shard_map/while/body/eval_jaxpr/conv_general_dilated | solution.py:25
  611.2 10.5 %copy.119 = bf16[32,4,32,7,16]{2,4,3,1,0:T(8,128)(2,1)} copy(bf16[32,4,32,7,16]{0,4,3,2,1:T(8,128)(2,1)} %bitcast.143) | data formatting | bytes 1835008 | tf_op jit(solution)/shard_map/while/body/eval_jaxpr/convert_element_type | solution.py:40
  624.8 10.4 %copy.117 = bf16[16,32,4,32,7]{3,0,4,2,1:T(8,128)(2,1)} copy(bf16[16,32,4,32,7]{1,0,4,3,2:T(8,128)(2,1)} %bitcast.145) | data formatting | bytes 1835008 | tf_op jit(solution)/shard_map/while/body/eval_jaxpr/conv_general_dilated | solution.py:25
  635.3 11.1 %convolution_select_fusion.3 = f32[32,4,32,5,1]{2,4,3,1,0:T(1,128)S(1)} fusion(bf16[16,32,4,32,7]{3,0,4,2,1:T(8,128)(2,1)} %copy.117, pred[32,5]{0,1:T(8,128)(4,1)S(1)} %get-tuple-element.250, bf16[1,16,3,3,3]{1,4,3,2,0:T(4,128)(2,1)S(1)} %get-tuple-element.215), kind=kOutput, calls=%fused_computation.23.clone.1 | convolution fusion | flops 14458880 | bytes 1000448 | tf_op jit(solution)/shard_map/while/body/eval_jaxpr/conv_general_dilated | solution.py:25
  646.3 8.9 %convolution_add_fusion.2 = f32[32,4,32,5,1]{2,4,3,1,0:T(1,128)S(1)} fusion(f32[32,4,32,5,1]{2,4,3,1,0:T(1,128)S(1)} %convolution_select_fusion.3, bf16[32,4,32,7,16]{2,4,3,1,0:T(8,128)(2,1)S(1)} %copy-done.2, bf16[1,16,3,3,3]{1,4,3,2,0:T(4,128)(2,1)S(1)} %get-tuple-element.219), kind=kOutput, calls=%fused_computation.18.clone.1 | convolution fusion | flops 14458880 | bytes 1082208 | tf_op jit(solution)/shard_map/while/body/eval_jaxpr/conv_general_dilated | solution.py:25
  655.3 10.0 %fusion.97 = f32[32,4,32,5,1]{2,4,3,1,0:T(1,128)S(1)} fusion(f32[32,4,32,5,1]{2,4,3,1,0:T(1,128)S(1)} %convolution_add_fusion.2, bf16[16,32,4,32,7]{3,0,4,2,1:T(8,128)(2,1)S(1)} %copy-done.1, pred[32,5]{0,1:T(8,128)(4,1)S(1)} %get-tuple-element.250, f32[]{:T(128)} %bitcast.141, bf16[1,16,3,3,3]{1,4,3,2,0:T(4,128)(2,1)S(1)} %get-tuple-element.221), kind=kOutput, calls=%fused_computation.22.clone.1 | convolution fusion | flops 14520320 | bytes 1082372 | tf_op jit(solution)/shard_map/while/body/eval_jaxpr/conv_general_dilated | solution.py:25
  (205 shorter events, 83.1 us)
Async XLA Ops:
  6.5 59.1 %all-gather.9.cloned.1.call-start = ((), (), s32[]{:S(2)}) async-start(), calls=%async_computation | async-start | bytes 4456448 | tf_op jit(solution)/shard_map/all_gather | solution.py:15
  12.4 104.4 %all-gather.11.cloned.1.call-start = ((), (), s32[]{:S(2)}) async-start(), calls=%async_computation.1 | async-start | bytes 4456448 | tf_op jit(solution)/shard_map/all_gather | solution.py:15
  13.2 154.7 %all-gather.13.cloned.1.call-start = ((), (), s32[]{:S(2)}) async-start(), calls=%async_computation.2 | async-start | bytes 4456448 | tf_op jit(solution)/shard_map/all_gather | solution.py:15
  13.9 204.9 %all-gather.15.cloned.1.call-start = ((), (), s32[]{:S(2)}) async-start(), calls=%async_computation.3 | async-start | bytes 4456448 | tf_op jit(solution)/shard_map/all_gather | solution.py:15
  171.0 51.4 %copy-start.5 = (bf16[128,1024]{1,0:T(8,128)(2,1)S(1)}, bf16[128,1024]{1,0:T(8,128)(2,1)}, u32[]{:S(2)}) copy-start(bf16[128,1024]{1,0:T(8,128)(2,1)} %param.10) | copy-start | bytes 786436
  218.8 4.3 copy-start.3
  218.8 4.3 copy-start.4
  218.9 4.3 copy-start.6
  218.9 4.3 copy-start.7
  276.1 10.5 %copy-start = (bf16[16,32,4,4,32]{1,0,4,3,2:T(8,128)(2,1)S(1)}, bf16[16,32,4,4,32]{1,0,4,3,2:T(8,128)(2,1)}, u32[]{:S(2)}) copy-start(bf16[16,32,4,4,32]{1,0,4,3,2:T(8,128)(2,1)} %get-tuple-element.214) | copy-start | bytes 1572868 | tf_op jit(solution)/shard_map/while
  300.1 11.1 %copy-start.2 = (bf16[32,4,32,7,16]{2,4,3,1,0:T(8,128)(2,1)S(1)}, bf16[32,4,32,7,16]{2,4,3,1,0:T(8,128)(2,1)}, u32[]{:S(2)}) copy-start(bf16[32,4,32,7,16]{2,4,3,1,0:T(8,128)(2,1)} %copy.119) | copy-start | bytes 2752516 | tf_op jit(solution)/shard_map/while
  311.2 9.0 %copy-start.1 = (bf16[16,32,4,32,7]{3,0,4,2,1:T(8,128)(2,1)S(1)}, bf16[16,32,4,32,7]{3,0,4,2,1:T(8,128)(2,1)}, u32[]{:S(2)}) copy-start(bf16[16,32,4,32,7]{3,0,4,2,1:T(8,128)(2,1)} %copy.120) | copy-start | bytes 2752516 | tf_op jit(solution)/shard_map/while
  387.7 10.5 %copy-start = (bf16[16,32,4,4,32]{1,0,4,3,2:T(8,128)(2,1)S(1)}, bf16[16,32,4,4,32]{1,0,4,3,2:T(8,128)(2,1)}, u32[]{:S(2)}) copy-start(bf16[16,32,4,4,32]{1,0,4,3,2:T(8,128)(2,1)} %get-tuple-element.214) | copy-start | bytes 1572868 | tf_op jit(solution)/shard_map/while
  411.8 11.3 %copy-start.2 = (bf16[32,4,32,7,16]{2,4,3,1,0:T(8,128)(2,1)S(1)}, bf16[32,4,32,7,16]{2,4,3,1,0:T(8,128)(2,1)}, u32[]{:S(2)}) copy-start(bf16[32,4,32,7,16]{2,4,3,1,0:T(8,128)(2,1)} %copy.119) | copy-start | bytes 2752516 | tf_op jit(solution)/shard_map/while
  423.1 9.0 %copy-start.1 = (bf16[16,32,4,32,7]{3,0,4,2,1:T(8,128)(2,1)S(1)}, bf16[16,32,4,32,7]{3,0,4,2,1:T(8,128)(2,1)}, u32[]{:S(2)}) copy-start(bf16[16,32,4,32,7]{3,0,4,2,1:T(8,128)(2,1)} %copy.120) | copy-start | bytes 2752516 | tf_op jit(solution)/shard_map/while
  499.6 10.5 %copy-start = (bf16[16,32,4,4,32]{1,0,4,3,2:T(8,128)(2,1)S(1)}, bf16[16,32,4,4,32]{1,0,4,3,2:T(8,128)(2,1)}, u32[]{:S(2)}) copy-start(bf16[16,32,4,4,32]{1,0,4,3,2:T(8,128)(2,1)} %get-tuple-element.214) | copy-start | bytes 1572868 | tf_op jit(solution)/shard_map/while
  523.6 11.0 %copy-start.2 = (bf16[32,4,32,7,16]{2,4,3,1,0:T(8,128)(2,1)S(1)}, bf16[32,4,32,7,16]{2,4,3,1,0:T(8,128)(2,1)}, u32[]{:S(2)}) copy-start(bf16[32,4,32,7,16]{2,4,3,1,0:T(8,128)(2,1)} %copy.119) | copy-start | bytes 2752516 | tf_op jit(solution)/shard_map/while
  534.7 9.0 %copy-start.1 = (bf16[16,32,4,32,7]{3,0,4,2,1:T(8,128)(2,1)S(1)}, bf16[16,32,4,32,7]{3,0,4,2,1:T(8,128)(2,1)}, u32[]{:S(2)}) copy-start(bf16[16,32,4,32,7]{3,0,4,2,1:T(8,128)(2,1)} %copy.120) | copy-start | bytes 2752516 | tf_op jit(solution)/shard_map/while
  611.2 10.5 %copy-start = (bf16[16,32,4,4,32]{1,0,4,3,2:T(8,128)(2,1)S(1)}, bf16[16,32,4,4,32]{1,0,4,3,2:T(8,128)(2,1)}, u32[]{:S(2)}) copy-start(bf16[16,32,4,4,32]{1,0,4,3,2:T(8,128)(2,1)} %get-tuple-element.214) | copy-start | bytes 1572868 | tf_op jit(solution)/shard_map/while
  635.3 11.1 %copy-start.2 = (bf16[32,4,32,7,16]{2,4,3,1,0:T(8,128)(2,1)S(1)}, bf16[32,4,32,7,16]{2,4,3,1,0:T(8,128)(2,1)}, u32[]{:S(2)}) copy-start(bf16[32,4,32,7,16]{2,4,3,1,0:T(8,128)(2,1)} %copy.119) | copy-start | bytes 2752516 | tf_op jit(solution)/shard_map/while
  646.3 9.0 %copy-start.1 = (bf16[16,32,4,32,7]{3,0,4,2,1:T(8,128)(2,1)S(1)}, bf16[16,32,4,32,7]{3,0,4,2,1:T(8,128)(2,1)}, u32[]{:S(2)}) copy-start(bf16[16,32,4,32,7]{3,0,4,2,1:T(8,128)(2,1)} %copy.120) | copy-start | bytes 2752516 | tf_op jit(solution)/shard_map/while
Sparse Core Ops, SparseCore 0:
  12.6 53.0 all-gather.8
  67.8 48.8 all-gather.10
  119.0 48.8 all-gather.12
  169.9 48.8 all-gather.14
